TPU v7x, 512 devices: a whole 4x8x8 slice. The times are simulated.
512 devices in a mesh: ctx: 32 (over y, x), fsdp: 16 (over z, core).
Axes of the slice: x: 4, y: 8, z: 8, core: 2. Of those that a mesh axis runs over, the one named last changes fastest.
Arguments:
- tokens: bfloat16 [131072, 4096], P(('ctx', 'fsdp')), may hold values from -48 to 48
- query_weight: bfloat16 [4096, 512], P('fsdp'), may hold values from -0.09375 to 0.09375
- key_weight: bfloat16 [4096, 128], P('fsdp'), may hold values from -0.09375 to 0.09375
- value_weight: bfloat16 [4096, 128], P('fsdp'), may hold values from -0.09375 to 0.09375
- chosen: int32 [256, 2], replicated, may hold values from 0 to 253, as said below
Outputs:
- attended: bfloat16 [131072, 512], P(('ctx', 'fsdp'))
Inputs may be any that keep to these rules, and one draw needn't show every extreme that they name: `chosen`: for query block q >= 3 both entries are distinct and below q - 1; block 2 names block 0 twice; blocks 0 and 1 name 0 twice, which selects nothing. The last block always selects block 253.
All inputs are finite; a program needn't handle non-finite values.
Results may differ from a plain program's by a relative error of at most 0.0065.
The roundings to bfloat16 on the way count: a program that leaves them out, or rounds other values in their place, can miss the bound.
Values may be sent and summed in bfloat16 or wider, within the bound.
No kernel may reach another device: no remote copies, remote signals or barrier semaphores. Data moves between devices by JAX's collectives and lax.ppermute only.
A program may use at most 64 MiB of HBM per device.

v0:
```python
import jax
import jax.numpy as jnp
from jax import lax
from jax.sharding import Mesh, PartitionSpec as P

QH = 4


def from_behind(array, axis, by):
    peers = lax.axis_size(axis)
    pairs = [(i, i + by) for i in range(peers) if 0 <= i + by < peers]
    return lax.ppermute(array, axis, pairs)


def gather_rows(array, axis):
    peers = lax.axis_size(axis)
    spread = jnp.broadcast_to(array[None], (peers,) + array.shape)
    got = lax.all_to_all(spread, axis, split_axis=0, concat_axis=0, tiled=True)
    return got.reshape((peers * array.shape[0],) + array.shape[1:])


def ring_gather_rows(array, axis, early_steps, tied):
    peers = lax.axis_size(axis)
    chips = peers // 2
    shift_pairs = lambda by: [(i, (i + by) % peers) for i in range(peers)]
    ahead = array
    behind = array
    from_ahead = []
    from_behind_ = []
    for step in range(chips // 2):
        if step == early_steps:
            ahead, behind, tied = lax.optimization_barrier((ahead, behind, tied))
            from_ahead[-1] = ahead
            if from_behind_:
                from_behind_[-1] = behind
        ahead = lax.ppermute(ahead, axis, shift_pairs(2))
        from_ahead.append(ahead)
        if step < chips // 2 - 1:
            behind = lax.ppermute(behind, axis, shift_pairs(-2))
            from_behind_.append(behind)
    mine = jnp.stack(from_ahead[::-1] + [array] + from_behind_, axis=0)
    other = lax.ppermute(mine, axis, [(i, i ^ 1) for i in range(peers)])
    lane = lax.axis_index(axis)
    start = (lane // 2 - chips // 2) % chips

    def natural(stacked):
        doubled = jnp.concatenate([stacked, stacked], axis=0)
        return lax.dynamic_slice_in_dim(doubled, chips - start, chips, 0)

    mine, other = (natural(mine), natural(other))
    core = lane % 2
    first = jnp.where(core == 0, mine, other)
    second = jnp.where(core == 0, other, mine)
    full = jnp.stack([first, second], axis=1)
    return (full.reshape((peers * array.shape[0],) + array.shape[1:]), tied)


def swap_partner(array, axis):
    peers = lax.axis_size(axis)
    pairs = [(i, i ^ 1) for i in range(peers)]
    return lax.ppermute(array, axis, pairs)


def per_device(tokens, query_weight, key_weight, value_weight, chosen):
    token_rows = tokens.shape[0]
    head_width = key_weight.shape[1]
    lane_count = lax.axis_size("fsdp")
    lane_index = lax.axis_index("fsdp")
    group_index = lax.axis_index(("cy", "cx"))
    blocks_group = lane_count // 2
    my_block = group_index * blocks_group + lane_index // 2
    global_index = group_index * lane_count + lane_index
    kv_weight = lax.all_gather(
        jnp.concatenate([key_weight, value_weight], axis=1), "fsdp", axis=0, tiled=True
    )
    q_weight, kv_weight = ring_gather_rows(query_weight, "fsdp", 2, kv_weight)
    kv_f32 = jnp.dot(tokens, kv_weight, preferred_element_type=jnp.float32)
    key_value = kv_f32.astype(jnp.bfloat16)
    along_x = lax.all_gather(key_value[None], "cx", axis=0, tiled=True)
    candidates = lax.all_gather(along_x[None], "cy", axis=0, tiled=True).reshape(
        (-1,) + key_value.shape
    )
    before_pair = from_behind(key_value, ("cy", "cx", "fsdp"), 1)
    own_block = jnp.concatenate([before_pair, key_value], axis=0)
    queries = jnp.dot(tokens, q_weight, preferred_element_type=jnp.float32)
    queries = queries.astype(jnp.bfloat16).reshape(token_rows, QH, head_width)
    queries, chosen = lax.optimization_barrier((queries, chosen))
    dest_block = group_index * blocks_group + jnp.arange(lane_count, dtype=jnp.int32) // 2
    dest_pick = chosen[dest_block, jnp.arange(lane_count, dtype=jnp.int32) % 2]
    outgoing = jnp.take(candidates, dest_pick // blocks_group, axis=0, mode="clip")
    incoming = lax.all_to_all(outgoing, "fsdp", split_axis=0, concat_axis=0, tiled=True)
    mine = lax.dynamic_index_in_dim(chosen, my_block, 0, keepdims=False)
    my_choice = lane_index % 2
    my_pick = jnp.where(my_choice == 0, mine[0], mine[1])
    place = my_pick % blocks_group * 2
    block_mine = lax.dynamic_slice_in_dim(incoming, place, 2, 0).reshape(
        2 * token_rows, 2 * head_width
    )
    block_partner = swap_partner(block_mine, "fsdp")
    scale = head_width ** (-0.5)
    scores = (
        jnp.concatenate(
            [
                jnp.einsum(
                    "qhd,kd->hqk", queries, rows[:, :head_width], preferred_element_type=jnp.float32
                )
                for rows in (own_block, block_mine, block_partner)
            ],
            axis=2,
        )
        * scale
    )
    value_rows = jnp.concatenate(
        [own_block[:, head_width:], block_mine[:, head_width:], block_partner[:, head_width:]],
        axis=0,
    )
    window_rows = own_block.shape[0]
    pick_rows = block_mine.shape[0]
    row_index = jnp.arange(token_rows, dtype=jnp.int32)
    column = jnp.arange(window_rows, dtype=jnp.int32)
    causal = (column[None, :] <= row_index[:, None] + token_rows) & (
        (column[None, :] >= token_rows) | (global_index > 0)
    )
    first_ok = mine[0] < my_block - 1
    second_ok = (mine[1] < my_block - 1) & (mine[1] != mine[0])
    mine_ok = jnp.where(my_choice == 0, first_ok, second_ok)
    partner_ok = jnp.where(my_choice == 0, second_ok, first_ok)
    visible = jnp.concatenate(
        [
            causal,
            jnp.broadcast_to(mine_ok, (token_rows, pick_rows)),
            jnp.broadcast_to(partner_ok, (token_rows, pick_rows)),
        ],
        axis=1,
    )
    scores = jnp.where(visible[None], scores, -jnp.inf)
    highest = jnp.max(scores, axis=2, keepdims=True)
    probs = jnp.exp(scores - highest)
    denominator = jnp.sum(probs, axis=2, keepdims=True)
    mixed = (
        jnp.einsum(
            "hqk,kd->hqd",
            probs.astype(jnp.bfloat16),
            value_rows,
            preferred_element_type=jnp.float32,
        )
        / denominator
    )
    return jnp.transpose(mixed, (1, 0, 2)).reshape(token_rows, -1).astype(jnp.bfloat16)


def split_ctx(mesh):
    column = mesh.devices[:, 0]
    coords = [getattr(device, "coords", None) for device in column]
    if any((c is None for c in coords)):
        across = 1
    else:
        across = len({c[0] for c in coords})
    groups, lanes = mesh.devices.shape
    return Mesh(mesh.devices.reshape(groups // across, across, lanes), ("cy", "cx", "fsdp"))


def solution(mesh):
    split = split_ctx(mesh)
    rows = P(("cy", "cx", "fsdp"), None)
    return jax.shard_map(
        per_device,
        mesh=split,
        in_specs=(rows, P("fsdp", None), P("fsdp", None), P("fsdp", None), P()),
        out_specs=rows,
        check_vma=False,
    )
```

profile of v0, /device:TPU:7, one launch (start us, length us, event | category | flops | bytes accessed | tf_op | source)
XLA Modules:
  0.0 211.8 jit_solution(5109586770303646003)
XLA Ops:
  6.5 1.7 pad_maximum_fusion.2
  8.3 4.1 %collective-permute-start = (bf16[256,512]{1,0:T(8,128)(2,1)}, bf16[256,512]{1,0:T(8,128)(2,1)S(1)}, u32[]{:S(2)}, u32[]{:S(2)}) collective-permute-start(bf16[256,512]{1,0:T(8,128)(2,1)} %param.6), channel_id=1, source_target_pairs={{0,2},{1,3},{2,4},{3,5},{4,6},{5,7},{6,8},{7,9},{8,10},{9,11},{10,... | collective-permute-start | bytes 786440 | tf_op jit(solution)/shard_map/ppermute | solution.py:36
  12.5 8.6 %collective-permute-start.2 = (bf16[256,512]{1,0:T(8,128)(2,1)}, bf16[256,512]{1,0:T(8,128)(2,1)S(1)}, u32[]{:S(2)}, u32[]{:S(2)}) collective-permute-start(bf16[256,512]{1,0:T(8,128)(2,1)} %param.6), channel_id=1, source_target_pairs={{0,14},{1,15},{2,0},{3,1},{4,2},{5,3},{6,4},{7,5},{8,6},{9,7},{10,... | collective-permute-start | bytes 786440 | tf_op jit(solution)/shard_map/ppermute | solution.py:39
  21.1 4.3 %collective-permute-done = bf16[256,512]{1,0:T(8,128)(2,1)S(1)} collective-permute-done((bf16[256,512]{1,0:T(8,128)(2,1)}, bf16[256,512]{1,0:T(8,128)(2,1)S(1)}, u32[]{:S(2)}, u32[]{:S(2)}) %collective-permute-start) | collective-permute-done | bytes 262176 | tf_op jit(solution)/shard_map/ppermute | solution.py:36
  25.4 1.9 collective-permute-start.1
  27.3 4.6 %collective-permute-start.3 = (bf16[256,512]{1,0:T(8,128)(2,1)S(1)}, bf16[256,512]{1,0:T(8,128)(2,1)S(1)}, u32[]{:S(2)}, u32[]{:S(2)}) collective-permute-start(bf16[256,512]{1,0:T(8,128)(2,1)S(1)} %collective-permute-done.2), channel_id=1, source_target_pairs={{0,14},{1,15},{2,0},{3,1},{4,2},{5,3},{6,4},{7,5},{8,6},{9,7},{10,... | collective-permute-start | bytes 786440 | tf_op jit(solution)/shard_map/ppermute | solution.py:39
  31.9 5.2 %collective-permute-done.1 = bf16[256,512]{1,0:T(8,128)(2,1)S(1)} collective-permute-done((bf16[256,512]{1,0:T(8,128)(2,1)S(1)}, bf16[256,512]{1,0:T(8,128)(2,1)S(1)}, u32[]{:S(2)}, u32[]{:S(2)}) %collective-permute-start.1) | collective-permute-done | bytes 262176 | tf_op jit(solution)/shard_map/ppermute | solution.py:36
  37.2 20.6 %all-gather.5.cloned.1.call-done = bf16[4096,256]{1,0:T(8,128)(2,1)} async-done(((bf16[256,256]{1,0:T(8,128)(2,1)}), bf16[4096,256]{1,0:T(8,128)(2,1)}) %all-gather.5.cloned.1.call-update) | async-done | bytes 2097168 | tf_op jit(solution)/shard_map/all_gather | solution.py:73
  57.8 2.3 %fusion.16 = bf16[256,256]{1,0:T(8,128)(2,1)S(1)} fusion(bf16[256,4096]{1,0:T(8,128)(2,1)S(1)} %copy-done, bf16[4096,256]{1,0:T(8,128)(2,1)} %all-gather.5.cloned.1.call-done), kind=kOutput, calls=%fused_computation.24 | convolution fusion | flops 536936448 | bytes 4325376 | tf_op jit(solution)/shard_map/dot_general | solution.py:77
  60.1 10.6 %all-gather = bf16[1024,256]{1,0:T(8,128)(2,1)} all-gather(bf16[256,256]{1,0:T(8,128)(2,1)S(1)} %fusion.16), channel_id=2, replica_groups=mesh['cy'=8,'cx'=4,'fsdp'=16] {'cx'}, dimensions={0}, use_global_device_ids=true | all-gather | bytes 655360 | tf_op jit(solution)/shard_map/all_gather | solution.py:79
  70.8 3.0 %collective-permute-start.4 = (bf16[256,512]{1,0:T(8,128)(2,1)S(1)}, bf16[256,512]{1,0:T(8,128)(2,1)S(1)}, u32[]{:S(2)}, u32[]{:S(2)}) collective-permute-start(bf16[256,512]{1,0:T(8,128)(2,1)S(1)} %collective-permute-done.1), channel_id=1, source_target_pairs={{0,2},{1,3},{2,4},{3,5},{4,6},{5,7},{6,8},{7,9},{8,10},{9,11},{10,... | collective-permute-start | bytes 786440 | tf_op jit(solution)/shard_map/ppermute | solution.py:36
  73.8 5.3 %collective-permute-done.4 = bf16[256,512]{1,0:T(8,128)(2,1)S(1)} collective-permute-done((bf16[256,512]{1,0:T(8,128)(2,1)S(1)}, bf16[256,512]{1,0:T(8,128)(2,1)S(1)}, u32[]{:S(2)}, u32[]{:S(2)}) %collective-permute-start.4) | collective-permute-done | bytes 262176 | tf_op jit(solution)/shard_map/ppermute | solution.py:36
  79.1 1.9 collective-permute-start.5
  81.0 4.6 %collective-permute-start.6 = (bf16[256,512]{1,0:T(8,128)(2,1)S(1)}, bf16[256,512]{1,0:T(8,128)(2,1)S(1)}, u32[]{:S(2)}, u32[]{:S(2)}) collective-permute-start(bf16[256,512]{1,0:T(8,128)(2,1)S(1)} %collective-permute-done.3), channel_id=1, source_target_pairs={{0,14},{1,15},{2,0},{3,1},{4,2},{5,3},{6,4},{7,5},{8,6},{9,7},{10,... | collective-permute-start | bytes 786440 | tf_op jit(solution)/shard_map/ppermute | solution.py:39
  85.6 1.8 collective-permute-done.5
  87.4 0.9 bitcast_dynamic-update-slice_fusion.22
  88.3 0.8 bitcast_dynamic-update-slice_fusion.19
  89.1 0.8 bitcast_dynamic-update-slice_fusion.16
  90.0 0.8 bitcast_dynamic-update-slice_fusion.13
  90.8 0.8 bitcast_dynamic-update-slice_fusion.10
  91.6 0.8 bitcast_dynamic-update-slice_fusion.7
  92.5 0.8 bitcast_dynamic-update-slice_fusion.4
  94.0 0.8 bitcast_dynamic-update-slice_fusion.1
  94.9 7.6 %collective-permute-start.7 = (bf16[8,256,512]{2,1,0:T(8,128)(2,1)}, bf16[8,256,512]{2,1,0:T(8,128)(2,1)}, u32[]{:S(2)}, u32[]{:S(2)}) collective-permute-start(bf16[8,256,512]{2,1,0:T(8,128)(2,1)} %get-tuple-element.17), channel_id=1, source_target_pairs={{0,1},{1,0},{2,3},{3,2},{4,5},{5,4},{6,7},{7,6},{8,9},{9,8},{10,11... | collective-permute-start | bytes 6291464 | tf_op jit(solution)/shard_map/ppermute | solution.py:42
  102.5 1.7 bitcast_dynamic-update-slice_fusion.23
  104.2 1.7 bitcast_dynamic-update-slice_fusion.20
  105.9 0.7 bitcast_dynamic-update-slice_fusion.17
  106.6 0.7 bitcast_dynamic-update-slice_fusion.14
  107.3 0.7 bitcast_dynamic-update-slice_fusion.11
  108.0 0.7 bitcast_dynamic-update-slice_fusion.8
  108.7 0.7 bitcast_dynamic-update-slice_fusion.5
  109.5 1.7 bitcast_dynamic-update-slice_fusion.2
  111.2 4.5 %select_bitcast_fusion.1 = (bf16[8,1,256,512]{3,2,1,0:T(8,128)(2,1)S(1)}, bf16[8,1,256,512]{3,2,1,0:T(8,128)(2,1)S(1)}) fusion(pred[]{:T(512)S(6)} %eq.14, bf16[16,256,512]{2,1,0:T(8,128)(2,1)} %bitcast_dynamic-update-slice_fusion.2, s32[]{:T(128)S(6)} %select_n.118, bf16[8,256,512]{2,1,0:T(8,128)(2,1)} %collective-permute-done.7), kind=kLoop, calls=%fused_computation.14 | loop fusion | flops 4194304 | bytes 8388613 | tf_op jit(solution)/shard_map/stack | solution.py:54
  116.1 1.3 convolution_convert_fusion
  118.2 11.0 %all-gather.7.cloned.1.call-done = bf16[32,256,256]{2,1,0:T(8,128)(2,1)} async-done(((bf16[4,256,256]{2,1,0:T(8,128)(2,1)}), bf16[32,256,256]{2,1,0:T(8,128)(2,1)}) %all-gather.7.cloned.1.call-update) | async-done | bytes 4194320 | tf_op jit(solution)/shard_map/all_gather | solution.py:80
  129.2 4.2 %gather_fusion.1 = bf16[16,256,256]{2,1,0:T(8,128)(2,1)} fusion(bf16[32,256,256]{2,1,0:T(8,128)(2,1)} %all-gather.7.cloned.1.call-done, s32[1024]{0:T(1024)S(1)} %pad_clamp_fusion), kind=kCustom, calls=%fused_computation.1 | custom fusion | bytes 4194368 | tf_op jit(solution)/shard_map/jit(_take)/gather | solution.py:90
  133.4 8.1 %all-to-all-start = ((bf16[16,256,256]{2,1,0:T(8,128)(2,1)}), bf16[16,256,256]{2,1,0:T(8,128)(2,1)}, u32[]{:S(2)}, u32[]{:S(2)}) async-start(bf16[16,256,256]{2,1,0:T(8,128)(2,1)} %gather_fusion.1), calls=%async_computation | async-start | bytes 4194304 | tf_op jit(solution)/shard_map/all_to_all | solution.py:91
  141.6 3.5 %collective-permute-start.8 = (bf16[256,256]{1,0:T(8,128)(2,1)S(1)}, bf16[256,256]{1,0:T(8,128)(2,1)S(1)}, u32[]{:S(2)}, u32[]{:S(2)}) collective-permute-start(bf16[256,256]{1,0:T(8,128)(2,1)S(1)} %fusion.16), channel_id=1, source_target_pairs={{0,1},{1,2},{2,3},{3,4},{4,5},{5,6},{6,7},{7,8},{8,9},{9,10},{10,1... | collective-permute-start | bytes 393224 | tf_op jit(solution)/shard_map/ppermute | solution.py:12
  149.5 39.2 %collective-permute-done.8 = bf16[256,256]{1,0:T(8,128)(2,1)S(1)} collective-permute-done((bf16[256,256]{1,0:T(8,128)(2,1)S(1)}, bf16[256,256]{1,0:T(8,128)(2,1)S(1)}, u32[]{:S(2)}, u32[]{:S(2)}) %collective-permute-start.8) | collective-permute-done | bytes 131104 | tf_op jit(solution)/shard_map/ppermute | solution.py:12
  188.7 1.7 convolution_bitcast_fusion.2
  190.4 1.4 add_add_fusion
  191.8 1.1 constant_dynamic-slice_fusion
  193.0 5.8 %collective-permute-start.9 = (bf16[512,256]{1,0:T(8,128)(2,1)S(1)}, bf16[512,256]{1,0:T(8,128)(2,1)S(1)}, u32[]{:S(2)}, u32[]{:S(2)}) collective-permute-start(bf16[512,256]{1,0:T(8,128)(2,1)S(1)} %bitcast.100), channel_id=1, source_target_pairs={{0,1},{1,0},{2,3},{3,2},{4,5},{5,4},{6,7},{7,6},{8,9},{9,8},{10,11... | collective-permute-start | bytes 786440 | tf_op jit(solution)/shard_map/ppermute | solution.py:61
  199.2 0.7 collective-permute-done.9
  200.3 0.8 fusion.18
  201.1 1.4 fusion.1
  202.5 1.6 fusion.13
  204.1 0.8 copy.25
  (41 shorter events, 3.7 us)
Async XLA Ops:
  6.5 51.3 %copy-start = (bf16[256,4096]{1,0:T(8,128)(2,1)S(1)}, bf16[256,4096]{1,0:T(8,128)(2,1)}, u32[]{:S(2)}) copy-start(bf16[256,4096]{1,0:T(8,128)(2,1)} %param.5) | copy-start | bytes 6291460
  6.5 51.3 %all-gather.5.cloned.1.call-start = ((), (), s32[]{:S(2)}) async-start(), calls=%async_computation.1 | async-start | bytes 2228224 | tf_op jit(solution)/shard_map/all_gather | solution.py:73
  8.3 82.6 %copy-start.3 = (bf16[256,512]{1,0:T(8,128)(2,1)S(1)}, bf16[256,512]{1,0:T(8,128)(2,1)}, u32[]{:S(2)}) copy-start(bf16[256,512]{1,0:T(8,128)(2,1)} %param.6) | copy-start | bytes 786436
  8.3 120.9 %all-gather.7.cloned.1.call-start = ((), (), s32[]{:S(2)}) async-start(), calls=%async_computation.2 | async-start | bytes 4718592 | tf_op jit(solution)/shard_map/all_gather | solution.py:80
  8.3 17.0 %collective-permute-start = (bf16[256,512]{1,0:T(8,128)(2,1)}, bf16[256,512]{1,0:T(8,128)(2,1)S(1)}, u32[]{:S(2)}, u32[]{:S(2)}) collective-permute-start(bf16[256,512]{1,0:T(8,128)(2,1)} %param.6), channel_id=1, source_target_pairs={{0,2},{1,3},{2,4},{3,5},{4,6},{5,7},{6,8},{7,9},{8,10},{9,11},{10,... | collective-permute-start | bytes 786440 | tf_op jit(solution)/shard_map/ppermute | solution.py:36
  12.5 14.8 %collective-permute-start.2 = (bf16[256,512]{1,0:T(8,128)(2,1)}, bf16[256,512]{1,0:T(8,128)(2,1)S(1)}, u32[]{:S(2)}, u32[]{:S(2)}) collective-permute-start(bf16[256,512]{1,0:T(8,128)(2,1)} %param.6), channel_id=1, source_target_pairs={{0,14},{1,15},{2,0},{3,1},{4,2},{5,3},{6,4},{7,5},{8,6},{9,7},{10,... | collective-permute-start | bytes 786440 | tf_op jit(solution)/shard_map/ppermute | solution.py:39
  25.4 11.7 %collective-permute-start.1 = (bf16[256,512]{1,0:T(8,128)(2,1)S(1)}, bf16[256,512]{1,0:T(8,128)(2,1)S(1)}, u32[]{:S(2)}, u32[]{:S(2)}) collective-permute-start(bf16[256,512]{1,0:T(8,128)(2,1)S(1)} %collective-permute-done), channel_id=1, source_target_pairs={{0,2},{1,3},{2,4},{3,5},{4,6},{5,7},{6,8},{7,9},{8,10},{9,11},{10,... | collective-permute-start | bytes 786440 | tf_op jit(solution)/shard_map/ppermute | solution.py:36
  27.3 9.9 %collective-permute-start.3 = (bf16[256,512]{1,0:T(8,128)(2,1)S(1)}, bf16[256,512]{1,0:T(8,128)(2,1)S(1)}, u32[]{:S(2)}, u32[]{:S(2)}) collective-permute-start(bf16[256,512]{1,0:T(8,128)(2,1)S(1)} %collective-permute-done.2), channel_id=1, source_target_pairs={{0,14},{1,15},{2,0},{3,1},{4,2},{5,3},{6,4},{7,5},{8,6},{9,7},{10,... | collective-permute-start | bytes 786440 | tf_op jit(solution)/shard_map/ppermute | solution.py:39
  70.8 8.3 %collective-permute-start.4 = (bf16[256,512]{1,0:T(8,128)(2,1)S(1)}, bf16[256,512]{1,0:T(8,128)(2,1)S(1)}, u32[]{:S(2)}, u32[]{:S(2)}) collective-permute-start(bf16[256,512]{1,0:T(8,128)(2,1)S(1)} %collective-permute-done.1), channel_id=1, source_target_pairs={{0,2},{1,3},{2,4},{3,5},{4,6},{5,7},{6,8},{7,9},{8,10},{9,11},{10,... | collective-permute-start | bytes 786440 | tf_op jit(solution)/shard_map/ppermute | solution.py:36
  79.1 15.8 %copy-start.5 = (bf16[256,512]{1,0:T(8,128)(2,1)}, bf16[256,512]{1,0:T(8,128)(2,1)S(1)}, u32[]{:S(2)}) copy-start(bf16[256,512]{1,0:T(8,128)(2,1)S(1)} %collective-permute-done.4) | copy-start | bytes 786436
  79.1 8.3 %collective-permute-start.5 = (bf16[256,512]{1,0:T(8,128)(2,1)S(1)}, bf16[256,512]{1,0:T(8,128)(2,1)S(1)}, u32[]{:S(2)}, u32[]{:S(2)}) collective-permute-start(bf16[256,512]{1,0:T(8,128)(2,1)S(1)} %collective-permute-done.4), channel_id=1, source_target_pairs={{0,2},{1,3},{2,4},{3,5},{4,6},{5,7},{6,8},{7,9},{8,10},{9,11},{10,... | collective-permute-start | bytes 786440 | tf_op jit(solution)/shard_map/ppermute | solution.py:36
  81.0 12.3 %collective-permute-start.6 = (bf16[256,512]{1,0:T(8,128)(2,1)S(1)}, bf16[256,512]{1,0:T(8,128)(2,1)S(1)}, u32[]{:S(2)}, u32[]{:S(2)}) collective-permute-start(bf16[256,512]{1,0:T(8,128)(2,1)S(1)} %collective-permute-done.3), channel_id=1, source_target_pairs={{0,14},{1,15},{2,0},{3,1},{4,2},{5,3},{6,4},{7,5},{8,6},{9,7},{10,... | collective-permute-start | bytes 786440 | tf_op jit(solution)/shard_map/ppermute | solution.py:39
  87.4 7.4 %copy-start.6 = (bf16[256,512]{1,0:T(8,128)(2,1)}, bf16[256,512]{1,0:T(8,128)(2,1)S(1)}, u32[]{:S(2)}) copy-start(bf16[256,512]{1,0:T(8,128)(2,1)S(1)} %collective-permute-done.5) | copy-start | bytes 786436
  93.3 0.7 copy-start.4
  94.9 16.3 %collective-permute-start.7 = (bf16[8,256,512]{2,1,0:T(8,128)(2,1)}, bf16[8,256,512]{2,1,0:T(8,128)(2,1)}, u32[]{:S(2)}, u32[]{:S(2)}) collective-permute-start(bf16[8,256,512]{2,1,0:T(8,128)(2,1)} %get-tuple-element.17), channel_id=1, source_target_pairs={{0,1},{1,0},{2,3},{3,2},{4,5},{5,4},{6,7},{7,6},{8,9},{9,8},{10,11... | collective-permute-start | bytes 6291464 | tf_op jit(solution)/shard_map/ppermute | solution.py:42
  116.1 1.3 copy-start.1
  133.4 58.4 %all-to-all-start = ((bf16[16,256,256]{2,1,0:T(8,128)(2,1)}), bf16[16,256,256]{2,1,0:T(8,128)(2,1)}, u32[]{:S(2)}, u32[]{:S(2)}) async-start(bf16[16,256,256]{2,1,0:T(8,128)(2,1)} %gather_fusion.1), calls=%async_computation | async-start | bytes 4194304 | tf_op jit(solution)/shard_map/all_to_all | solution.py:91
  141.6 47.0 %collective-permute-start.8 = (bf16[256,256]{1,0:T(8,128)(2,1)S(1)}, bf16[256,256]{1,0:T(8,128)(2,1)S(1)}, u32[]{:S(2)}, u32[]{:S(2)}) collective-permute-start(bf16[256,256]{1,0:T(8,128)(2,1)S(1)} %fusion.16), channel_id=1, source_target_pairs={{0,1},{1,2},{2,3},{3,4},{4,5},{5,6},{6,7},{7,8},{8,9},{9,10},{10,1... | collective-permute-start | bytes 393224 | tf_op jit(solution)/shard_map/ppermute | solution.py:12
  191.8 8.5 %copy-start.2 = (f32[4,256,512]{1,2,0:T(8,128)S(1)}, f32[4,256,512]{1,2,0:T(8,128)}, u32[]{:S(2)}) copy-start(f32[4,256,512]{1,2,0:T(8,128)} %convolution_bitcast_fusion.2) | copy-start | bytes 6291460
  193.0 6.9 %collective-permute-start.9 = (bf16[512,256]{1,0:T(8,128)(2,1)S(1)}, bf16[512,256]{1,0:T(8,128)(2,1)S(1)}, u32[]{:S(2)}, u32[]{:S(2)}) collective-permute-start(bf16[512,256]{1,0:T(8,128)(2,1)S(1)} %bitcast.100), channel_id=1, source_target_pairs={{0,1},{1,0},{2,3},{3,2},{4,5},{5,4},{6,7},{7,6},{8,9},{9,8},{10,11... | collective-permute-start | bytes 786440 | tf_op jit(solution)/shard_map/ppermute | solution.py:61
Sparse Core Ops, SparseCore 0:
  9.5 48.2 all-gather.4
  70.9 58.2 all-gather.6
where the time goes:
time: 212 us
  waiting for transfers between devices  88.3 us (42%)
  starting transfers between devices  53.7 us (25%)
  local copies, waits for them, and re-layouts  23.6 us (11%)
  between operations  17.4 us (8%)
  blocking collectives  10.6 us (5%)
  other arithmetic  10.4 us (5%)
  matrix products  7.73 us (4%)
    ppermute x1, waiting for transfers between devices, from_behind(): return lax.ppermute(array, axis, pairs)  39.2 us
    all_gather x1, waiting for transfers between devices, per_device(): lax.all_gather(jnp.concatenate([key_weight, value_weight], axis=1), 'fsdp...  20.6 us
    ppermute x3, starting transfers between devices, ring_gather_rows(): behind = lax.ppermute(behind, axis, shift_pairs(-2))  17.7 us
    ppermute x4, waiting for transfers between devices, ring_gather_rows(): ahead = lax.ppermute(ahead, axis, shift_pairs(2))  16.6 us
    unnamed x28, local copies, waits for them, and re-layouts  13.6 us
    all_gather x1, waiting for transfers between devices, per_device(): lax.all_gather(along_x[None], 'cy', axis=0, tiled=True)  11 us
    ppermute x4, starting transfers between devices, ring_gather_rows(): ahead = lax.ppermute(ahead, axis, shift_pairs(2))  11 us
    all_gather x1, blocking collectives, per_device(): along_x = lax.all_gather(key_value[None], 'cx', axis=0, tiled=True)  10.6 us
  transfers between devices with their start and end apart: 13, of which 9 were waited for; matrix products, arithmetic and copies ran while one was open for 13% of the time, Pallas kernels for 0%

commit v1 on v0

--- a/solution.py
+++ b/solution.py
@@ -4,6 +4,12 @@
 from jax.sharding import Mesh, PartitionSpec as P
 
 QH = 4
+
+
+def gather_by_exchange(x, axis, dim):
+    count = lax.axis_size(axis)
+    repeats = [count if d == dim else 1 for d in range(x.ndim)]
+    return lax.all_to_all(jnp.tile(x, repeats), axis, split_axis=dim, concat_axis=dim, tiled=True)
 
 
 def from_behind(array, axis, by):
@@ -70,9 +76,7 @@
     blocks_group = lane_count // 2
     my_block = group_index * blocks_group + lane_index // 2
     global_index = group_index * lane_count + lane_index
-    kv_weight = lax.all_gather(
-        jnp.concatenate([key_weight, value_weight], axis=1), "fsdp", axis=0, tiled=True
-    )
+    kv_weight = gather_by_exchange(jnp.concatenate([key_weight, value_weight], axis=1), "fsdp", 0)
     q_weight, kv_weight = ring_gather_rows(query_weight, "fsdp", 2, kv_weight)
     kv_f32 = jnp.dot(tokens, kv_weight, preferred_element_type=jnp.float32)
     key_value = kv_f32.astype(jnp.bfloat16)

time: 212 us -> 244 us (1.15)
  waiting for transfers between devices: 88.3 us -> 113 us
  starting transfers between devices: 53.7 us -> 58.2 us
    ppermute x4, waiting for transfers between devices: 16.6 us -> 60.1 us  [ring_gather_rows(): ahead = lax.ppermute(ahead, axis, shift_pairs(2))]
    all_gather x1 -> x0, waiting for transfers between devices: 20.6 us -> none  [per_device(): lax.all_gather(jnp.concatenate([key_weight, value_weight], axis=1), 'fsdp...]
    all_to_all x0 -> x1, starting transfers between devices: none -> 11 us  [gather_by_exchange(): lax.all_to_all(jnp.tile(x, repeats), axis, split_axis=dim, concat_axis=di...]
    ppermute x3, starting transfers between devices: 17.7 us -> 12.3 us  [ring_gather_rows(): behind = lax.ppermute(behind, axis, shift_pairs(-2))]
  transfers between devices with their start and end apart: 13 -> 13, of which waited for: 9 -> 8; matrix products, arithmetic and copies ran while one was open for 13% -> 11% of each run, Pallas kernels for 0% -> 0%
where the time goes in v1:
time: 244 us; the launch traced here: 243 us
  waiting for transfers between devices  113 us (46%)
  starting transfers between devices  58.2 us (24%)
  local copies, waits for them, and re-layouts  25.2 us (10%)
  between operations  17.6 us (7%)
  blocking collectives  11.3 us (5%)
  other arithmetic  9.71 us (4%)
  matrix products  7.73 us (3%)
    ppermute x4, waiting for transfers between devices, ring_gather_rows(): ahead = lax.ppermute(ahead, axis, shift_pairs(2))  60.1 us
    ppermute x1, waiting for transfers between devices, from_behind(): return lax.ppermute(array, axis, pairs)  39 us
    unnamed x28, local copies, waits for them, and re-layouts  13.6 us
    all_gather x1, waiting for transfers between devices, per_device(): lax.all_gather(along_x[None], 'cy', axis=0, tiled=True)  12.5 us
    ppermute x3, starting transfers between devices, ring_gather_rows(): behind = lax.ppermute(behind, axis, shift_pairs(-2))  12.3 us
    all_gather x1, blocking collectives, per_device(): along_x = lax.all_gather(key_value[None], 'cx', axis=0, tiled=True)  11.3 us
    all_to_all x1, starting transfers between devices, gather_by_exchange(): lax.all_to_all(jnp.tile(x, repeats), axis, split_axis=dim, concat_axis=di...  11 us
    ppermute x4, starting transfers between devices, ring_gather_rows(): ahead = lax.ppermute(ahead, axis, shift_pairs(2))  9.03 us
  transfers between devices with their start and end apart: 13, of which 8 were waited for; matrix products, arithmetic and copies ran while one was open for 11% of the time, Pallas kernels for 0%

profile of v1, /device:TPU:7, one launch (start us, length us, event | category | flops | bytes accessed | tf_op | source)
XLA Modules:
  0.0 242.9 jit_solution(7440796818933710011)
XLA Ops:
  6.5 1.0 pad_maximum_fusion.2
  7.6 1.5 tile.2
  9.1 11.0 %all-to-all-start = ((bf16[16,256,256]{2,1,0:T(8,128)(2,1)}), bf16[16,256,256]{2,1,0:T(8,128)(2,1)}, u32[]{:S(2)}, u32[]{:S(2)}) async-start(bf16[16,256,256]{2,1,0:T(8,128)(2,1)} %tile.2), calls=%async_computation | async-start | bytes 4194304 | tf_op jit(solution)/shard_map/all_to_all | solution.py:12
  20.2 3.3 %collective-permute-start = (bf16[256,512]{1,0:T(8,128)(2,1)S(1)}, bf16[256,512]{1,0:T(8,128)(2,1)S(1)}, u32[]{:S(2)}, u32[]{:S(2)}) collective-permute-start(bf16[256,512]{1,0:T(8,128)(2,1)S(1)} %copy-done.3), channel_id=1, source_target_pairs={{0,2},{1,3},{2,4},{3,5},{4,6},{5,7},{6,8},{7,9},{8,10},{9,11},{10,... | collective-permute-start | bytes 786440 | tf_op jit(solution)/shard_map/ppermute | solution.py:42
  23.5 3.2 %collective-permute-start.2 = (bf16[256,512]{1,0:T(8,128)(2,1)S(1)}, bf16[256,512]{1,0:T(8,128)(2,1)S(1)}, u32[]{:S(2)}, u32[]{:S(2)}) collective-permute-start(bf16[256,512]{1,0:T(8,128)(2,1)S(1)} %copy-done.3), channel_id=1, source_target_pairs={{0,14},{1,15},{2,0},{3,1},{4,2},{5,3},{6,4},{7,5},{8,6},{9,7},{10,... | collective-permute-start | bytes 786440 | tf_op jit(solution)/shard_map/ppermute | solution.py:45
  26.7 47.6 %collective-permute-done = bf16[256,512]{1,0:T(8,128)(2,1)S(1)} collective-permute-done((bf16[256,512]{1,0:T(8,128)(2,1)S(1)}, bf16[256,512]{1,0:T(8,128)(2,1)S(1)}, u32[]{:S(2)}, u32[]{:S(2)}) %collective-permute-start) | collective-permute-done | bytes 262176 | tf_op jit(solution)/shard_map/ppermute | solution.py:42
  74.2 1.9 collective-permute-start.1
  76.2 4.6 %collective-permute-start.3 = (bf16[256,512]{1,0:T(8,128)(2,1)S(1)}, bf16[256,512]{1,0:T(8,128)(2,1)S(1)}, u32[]{:S(2)}, u32[]{:S(2)}) collective-permute-start(bf16[256,512]{1,0:T(8,128)(2,1)S(1)} %collective-permute-done.2), channel_id=1, source_target_pairs={{0,14},{1,15},{2,0},{3,1},{4,2},{5,3},{6,4},{7,5},{8,6},{9,7},{10,... | collective-permute-start | bytes 786440 | tf_op jit(solution)/shard_map/ppermute | solution.py:45
  80.7 3.5 %collective-permute-done.1 = bf16[256,512]{1,0:T(8,128)(2,1)S(1)} collective-permute-done((bf16[256,512]{1,0:T(8,128)(2,1)S(1)}, bf16[256,512]{1,0:T(8,128)(2,1)S(1)}, u32[]{:S(2)}, u32[]{:S(2)}) %collective-permute-start.1) | collective-permute-done | bytes 262176 | tf_op jit(solution)/shard_map/ppermute | solution.py:42
  84.3 0.9 collective-permute-done.3
  85.2 2.3 fusion.16
  87.5 11.3 %all-gather = bf16[1024,256]{1,0:T(8,128)(2,1)} all-gather(bf16[256,256]{1,0:T(8,128)(2,1)S(1)} %fusion.16), channel_id=2, replica_groups=mesh['cy'=8,'cx'=4,'fsdp'=16] {'cx'}, dimensions={0}, use_global_device_ids=true | all-gather | bytes 655360 | tf_op jit(solution)/shard_map/all_gather | solution.py:83
  98.8 1.9 collective-permute-start.4
  100.7 7.1 %collective-permute-done.4 = bf16[256,512]{1,0:T(8,128)(2,1)S(1)} collective-permute-done((bf16[256,512]{1,0:T(8,128)(2,1)S(1)}, bf16[256,512]{1,0:T(8,128)(2,1)S(1)}, u32[]{:S(2)}, u32[]{:S(2)}) %collective-permute-start.4) | collective-permute-done | bytes 262176 | tf_op jit(solution)/shard_map/ppermute | solution.py:42
  107.9 1.9 collective-permute-start.5
  109.8 4.6 %collective-permute-start.6 = (bf16[256,512]{1,0:T(8,128)(2,1)S(1)}, bf16[256,512]{1,0:T(8,128)(2,1)S(1)}, u32[]{:S(2)}, u32[]{:S(2)}) collective-permute-start(bf16[256,512]{1,0:T(8,128)(2,1)S(1)} %collective-permute-done.3), channel_id=1, source_target_pairs={{0,14},{1,15},{2,0},{3,1},{4,2},{5,3},{6,4},{7,5},{8,6},{9,7},{10,... | collective-permute-start | bytes 786440 | tf_op jit(solution)/shard_map/ppermute | solution.py:45
  114.4 1.8 collective-permute-done.5
  116.2 0.9 bitcast_dynamic-update-slice_fusion.22
  117.1 0.8 bitcast_dynamic-update-slice_fusion.19
  117.9 0.8 bitcast_dynamic-update-slice_fusion.16
  118.7 0.8 bitcast_dynamic-update-slice_fusion.13
  119.6 0.9 bitcast_dynamic-update-slice_fusion.10
  120.4 0.8 bitcast_dynamic-update-slice_fusion.7
  121.3 0.8 bitcast_dynamic-update-slice_fusion.4
  122.8 0.9 bitcast_dynamic-update-slice_fusion.1
  123.7 8.4 %collective-permute-start.7 = (bf16[8,256,512]{2,1,0:T(8,128)(2,1)}, bf16[8,256,512]{2,1,0:T(8,128)(2,1)}, u32[]{:S(2)}, u32[]{:S(2)}) collective-permute-start(bf16[8,256,512]{2,1,0:T(8,128)(2,1)} %get-tuple-element.17), channel_id=1, source_target_pairs={{0,1},{1,0},{2,3},{3,2},{4,5},{5,4},{6,7},{7,6},{8,9},{9,8},{10,11... | collective-permute-start | bytes 6291464 | tf_op jit(solution)/shard_map/ppermute | solution.py:48
  132.1 1.7 bitcast_dynamic-update-slice_fusion.23
  133.8 1.7 bitcast_dynamic-update-slice_fusion.20
  135.5 0.7 bitcast_dynamic-update-slice_fusion.17
  136.9 0.7 bitcast_dynamic-update-slice_fusion.11
  137.6 0.7 bitcast_dynamic-update-slice_fusion.8
  138.4 0.7 bitcast_dynamic-update-slice_fusion.5
  139.1 1.7 bitcast_dynamic-update-slice_fusion.2
  140.8 4.5 %select_bitcast_fusion.1 = (bf16[8,1,256,512]{3,2,1,0:T(8,128)(2,1)S(1)}, bf16[8,1,256,512]{3,2,1,0:T(8,128)(2,1)S(1)}) fusion(pred[]{:T(512)S(6)} %eq.14, bf16[16,256,512]{2,1,0:T(8,128)(2,1)} %bitcast_dynamic-update-slice_fusion.2, s32[]{:T(128)S(6)} %select_n.118, bf16[8,256,512]{2,1,0:T(8,128)(2,1)} %collective-permute-done.7), kind=kLoop, calls=%fused_computation.14 | loop fusion | flops 4194304 | bytes 8388613 | tf_op jit(solution)/shard_map/stack | solution.py:60
  145.8 1.3 convolution_convert_fusion
  147.8 12.5 %all-gather.4.cloned.1.call-done = bf16[32,256,256]{2,1,0:T(8,128)(2,1)} async-done(((bf16[4,256,256]{2,1,0:T(8,128)(2,1)}), bf16[32,256,256]{2,1,0:T(8,128)(2,1)}) %all-gather.4.cloned.1.call-update) | async-done | bytes 4194320 | tf_op jit(solution)/shard_map/all_gather | solution.py:84
  160.3 4.2 %gather_fusion.1 = bf16[16,256,256]{2,1,0:T(8,128)(2,1)} fusion(bf16[32,256,256]{2,1,0:T(8,128)(2,1)} %all-gather.4.cloned.1.call-done, s32[1024]{0:T(1024)S(1)} %pad_clamp_fusion), kind=kCustom, calls=%fused_computation.1 | custom fusion | bytes 4194368 | tf_op jit(solution)/shard_map/jit(_take)/gather | solution.py:94
  164.5 8.1 %all-to-all-start.1 = ((bf16[16,256,256]{2,1,0:T(8,128)(2,1)}), bf16[16,256,256]{2,1,0:T(8,128)(2,1)}, u32[]{:S(2)}, u32[]{:S(2)}) async-start(bf16[16,256,256]{2,1,0:T(8,128)(2,1)} %gather_fusion.1), calls=%async_computation.1 | async-start | bytes 4194304 | tf_op jit(solution)/shard_map/all_to_all | solution.py:95
  172.8 3.5 %collective-permute-start.8 = (bf16[256,256]{1,0:T(8,128)(2,1)S(1)}, bf16[256,256]{1,0:T(8,128)(2,1)S(1)}, u32[]{:S(2)}, u32[]{:S(2)}) collective-permute-start(bf16[256,256]{1,0:T(8,128)(2,1)S(1)} %fusion.16), channel_id=1, source_target_pairs={{0,1},{1,2},{2,3},{3,4},{4,5},{5,6},{6,7},{7,8},{8,9},{9,10},{10,1... | collective-permute-start | bytes 393224 | tf_op jit(solution)/shard_map/ppermute | solution.py:18
  180.8 39.0 %collective-permute-done.8 = bf16[256,256]{1,0:T(8,128)(2,1)S(1)} collective-permute-done((bf16[256,256]{1,0:T(8,128)(2,1)S(1)}, bf16[256,256]{1,0:T(8,128)(2,1)S(1)}, u32[]{:S(2)}, u32[]{:S(2)}) %collective-permute-start.8) | collective-permute-done | bytes 131104 | tf_op jit(solution)/shard_map/ppermute | solution.py:18
  219.8 1.7 convolution_bitcast_fusion.2
  221.5 1.4 add_add_fusion
  223.0 1.1 constant_dynamic-slice_fusion
  224.1 5.8 %collective-permute-start.9 = (bf16[512,256]{1,0:T(8,128)(2,1)S(1)}, bf16[512,256]{1,0:T(8,128)(2,1)S(1)}, u32[]{:S(2)}, u32[]{:S(2)}) collective-permute-start(bf16[512,256]{1,0:T(8,128)(2,1)S(1)} %bitcast.101), channel_id=1, source_target_pairs={{0,1},{1,0},{2,3},{3,2},{4,5},{5,4},{6,7},{7,6},{8,9},{9,8},{10,11... | collective-permute-start | bytes 786440 | tf_op jit(solution)/shard_map/ppermute | solution.py:67
  231.5 0.8 fusion.18
  232.2 1.4 fusion.1
  233.7 1.6 fusion.13
  235.2 0.8 copy.25
  (41 shorter events, 4.9 us)
Async XLA Ops:
  6.5 78.6 %copy-start = (bf16[256,4096]{1,0:T(8,128)(2,1)S(1)}, bf16[256,4096]{1,0:T(8,128)(2,1)}, u32[]{:S(2)}) copy-start(bf16[256,4096]{1,0:T(8,128)(2,1)} %param.5) | copy-start | bytes 6291460
  6.5 13.6 %copy-start.3 = (bf16[256,512]{1,0:T(8,128)(2,1)S(1)}, bf16[256,512]{1,0:T(8,128)(2,1)}, u32[]{:S(2)}) copy-start(bf16[256,512]{1,0:T(8,128)(2,1)} %param.6) | copy-start | bytes 786436
  9.1 76.1 %all-to-all-start = ((bf16[16,256,256]{2,1,0:T(8,128)(2,1)}), bf16[16,256,256]{2,1,0:T(8,128)(2,1)}, u32[]{:S(2)}, u32[]{:S(2)}) async-start(bf16[16,256,256]{2,1,0:T(8,128)(2,1)} %tile.2), calls=%async_computation | async-start | bytes 4194304 | tf_op jit(solution)/shard_map/all_to_all | solution.py:12
  20.1 140.2 %all-gather.4.cloned.1.call-start = ((), (), s32[]{:S(2)}) async-start(), calls=%async_computation.2 | async-start | bytes 4718592 | tf_op jit(solution)/shard_map/all_gather | solution.py:84
  20.2 54.1 %collective-permute-start = (bf16[256,512]{1,0:T(8,128)(2,1)S(1)}, bf16[256,512]{1,0:T(8,128)(2,1)S(1)}, u32[]{:S(2)}, u32[]{:S(2)}) collective-permute-start(bf16[256,512]{1,0:T(8,128)(2,1)S(1)} %copy-done.3), channel_id=1, source_target_pairs={{0,2},{1,3},{2,4},{3,5},{4,6},{5,7},{6,8},{7,9},{8,10},{9,11},{10,... | collective-permute-start | bytes 786440 | tf_op jit(solution)/shard_map/ppermute | solution.py:42
  23.5 52.7 %collective-permute-start.2 = (bf16[256,512]{1,0:T(8,128)(2,1)S(1)}, bf16[256,512]{1,0:T(8,128)(2,1)S(1)}, u32[]{:S(2)}, u32[]{:S(2)}) collective-permute-start(bf16[256,512]{1,0:T(8,128)(2,1)S(1)} %copy-done.3), channel_id=1, source_target_pairs={{0,14},{1,15},{2,0},{3,1},{4,2},{5,3},{6,4},{7,5},{8,6},{9,7},{10,... | collective-permute-start | bytes 786440 | tf_op jit(solution)/shard_map/ppermute | solution.py:45
  74.2 10.0 %collective-permute-start.1 = (bf16[256,512]{1,0:T(8,128)(2,1)S(1)}, bf16[256,512]{1,0:T(8,128)(2,1)S(1)}, u32[]{:S(2)}, u32[]{:S(2)}) collective-permute-start(bf16[256,512]{1,0:T(8,128)(2,1)S(1)} %collective-permute-done), channel_id=1, source_target_pairs={{0,2},{1,3},{2,4},{3,5},{4,6},{5,7},{6,8},{7,9},{8,10},{9,11},{10,... | collective-permute-start | bytes 786440 | tf_op jit(solution)/shard_map/ppermute | solution.py:42
  76.2 9.0 %collective-permute-start.3 = (bf16[256,512]{1,0:T(8,128)(2,1)S(1)}, bf16[256,512]{1,0:T(8,128)(2,1)S(1)}, u32[]{:S(2)}, u32[]{:S(2)}) collective-permute-start(bf16[256,512]{1,0:T(8,128)(2,1)S(1)} %collective-permute-done.2), channel_id=1, source_target_pairs={{0,14},{1,15},{2,0},{3,1},{4,2},{5,3},{6,4},{7,5},{8,6},{9,7},{10,... | collective-permute-start | bytes 786440 | tf_op jit(solution)/shard_map/ppermute | solution.py:45
  98.8 9.1 %collective-permute-start.4 = (bf16[256,512]{1,0:T(8,128)(2,1)S(1)}, bf16[256,512]{1,0:T(8,128)(2,1)S(1)}, u32[]{:S(2)}, u32[]{:S(2)}) collective-permute-start(bf16[256,512]{1,0:T(8,128)(2,1)S(1)} %collective-permute-done.1), channel_id=1, source_target_pairs={{0,2},{1,3},{2,4},{3,5},{4,6},{5,7},{6,8},{7,9},{8,10},{9,11},{10,... | collective-permute-start | bytes 786440 | tf_op jit(solution)/shard_map/ppermute | solution.py:42
  107.9 15.8 %copy-start.5 = (bf16[256,512]{1,0:T(8,128)(2,1)}, bf16[256,512]{1,0:T(8,128)(2,1)S(1)}, u32[]{:S(2)}) copy-start(bf16[256,512]{1,0:T(8,128)(2,1)S(1)} %collective-permute-done.4) | copy-start | bytes 786436
  107.9 8.3 %collective-permute-start.5 = (bf16[256,512]{1,0:T(8,128)(2,1)S(1)}, bf16[256,512]{1,0:T(8,128)(2,1)S(1)}, u32[]{:S(2)}, u32[]{:S(2)}) collective-permute-start(bf16[256,512]{1,0:T(8,128)(2,1)S(1)} %collective-permute-done.4), channel_id=1, source_target_pairs={{0,2},{1,3},{2,4},{3,5},{4,6},{5,7},{6,8},{7,9},{8,10},{9,11},{10,... | collective-permute-start | bytes 786440 | tf_op jit(solution)/shard_map/ppermute | solution.py:42
  109.8 12.3 %collective-permute-start.6 = (bf16[256,512]{1,0:T(8,128)(2,1)S(1)}, bf16[256,512]{1,0:T(8,128)(2,1)S(1)}, u32[]{:S(2)}, u32[]{:S(2)}) collective-permute-start(bf16[256,512]{1,0:T(8,128)(2,1)S(1)} %collective-permute-done.3), channel_id=1, source_target_pairs={{0,14},{1,15},{2,0},{3,1},{4,2},{5,3},{6,4},{7,5},{8,6},{9,7},{10,... | collective-permute-start | bytes 786440 | tf_op jit(solution)/shard_map/ppermute | solution.py:45
  116.2 7.5 %copy-start.6 = (bf16[256,512]{1,0:T(8,128)(2,1)}, bf16[256,512]{1,0:T(8,128)(2,1)S(1)}, u32[]{:S(2)}) copy-start(bf16[256,512]{1,0:T(8,128)(2,1)S(1)} %collective-permute-done.5) | copy-start | bytes 786436
  122.1 0.7 copy-start.4
  123.7 17.1 %collective-permute-start.7 = (bf16[8,256,512]{2,1,0:T(8,128)(2,1)}, bf16[8,256,512]{2,1,0:T(8,128)(2,1)}, u32[]{:S(2)}, u32[]{:S(2)}) collective-permute-start(bf16[8,256,512]{2,1,0:T(8,128)(2,1)} %get-tuple-element.17), channel_id=1, source_target_pairs={{0,1},{1,0},{2,3},{3,2},{4,5},{5,4},{6,7},{7,6},{8,9},{9,8},{10,11... | collective-permute-start | bytes 6291464 | tf_op jit(solution)/shard_map/ppermute | solution.py:48
  145.8 1.3 copy-start.1
  164.5 58.4 %all-to-all-start.1 = ((bf16[16,256,256]{2,1,0:T(8,128)(2,1)}), bf16[16,256,256]{2,1,0:T(8,128)(2,1)}, u32[]{:S(2)}, u32[]{:S(2)}) async-start(bf16[16,256,256]{2,1,0:T(8,128)(2,1)} %gather_fusion.1), calls=%async_computation.1 | async-start | bytes 4194304 | tf_op jit(solution)/shard_map/all_to_all | solution.py:95
  172.8 47.0 %collective-permute-start.8 = (bf16[256,256]{1,0:T(8,128)(2,1)S(1)}, bf16[256,256]{1,0:T(8,128)(2,1)S(1)}, u32[]{:S(2)}, u32[]{:S(2)}) collective-permute-start(bf16[256,256]{1,0:T(8,128)(2,1)S(1)} %fusion.16), channel_id=1, source_target_pairs={{0,1},{1,2},{2,3},{3,4},{4,5},{5,6},{6,7},{7,8},{8,9},{9,10},{10,1... | collective-permute-start | bytes 393224 | tf_op jit(solution)/shard_map/ppermute | solution.py:18
  223.0 8.5 %copy-start.2 = (f32[4,256,512]{1,2,0:T(8,128)S(1)}, f32[4,256,512]{1,2,0:T(8,128)}, u32[]{:S(2)}) copy-start(f32[4,256,512]{1,2,0:T(8,128)} %convolution_bitcast_fusion.2) | copy-start | bytes 6291460
  224.1 6.9 %collective-permute-start.9 = (bf16[512,256]{1,0:T(8,128)(2,1)S(1)}, bf16[512,256]{1,0:T(8,128)(2,1)S(1)}, u32[]{:S(2)}, u32[]{:S(2)}) collective-permute-start(bf16[512,256]{1,0:T(8,128)(2,1)S(1)} %bitcast.101), channel_id=1, source_target_pairs={{0,1},{1,0},{2,3},{3,2},{4,5},{5,4},{6,7},{7,6},{8,9},{9,8},{10,11... | collective-permute-start | bytes 786440 | tf_op jit(solution)/shard_map/ppermute | solution.py:67
Sparse Core Ops, SparseCore 0:
  98.9 61.3 all-gather.3
